TPU v7x, 128 devices: a whole 4x4x4 slice. The times are simulated.
128 devices in a mesh: shards: 8 (over x, core), tensor: 4 (over z), section: 4 (over y).
Axes of the slice: x: 4, y: 4, z: 4, core: 2. Of those that a mesh axis runs over, the one named last changes fastest.
Arguments:
- attn_grad: bfloat16 [16, 4, 1024, 1024], P('section', None, 'shards', 'tensor'), may hold values from -60 to 60
- mlp_in_grad: bfloat16 [16, 2, 1024, 2816], P('section', None, 'shards', 'tensor'), may hold values from -60 to 60
- mlp_out_grad: bfloat16 [16, 2816, 1024], P('section', 'tensor', 'shards'), may hold values from -60 to 60
- attn_momentum: bfloat16 [16, 4, 1024, 1024], P('section', None, 'shards', 'tensor'), may hold values from -3 to 3
- mlp_in_momentum: bfloat16 [16, 2, 1024, 2816], P('section', None, 'shards', 'tensor'), may hold values from -3 to 3
- mlp_out_momentum: bfloat16 [16, 2816, 1024], P('section', 'tensor', 'shards'), may hold values from -3 to 3
- owners: int32 [16, 7], P('section'), may hold values from 0 to 31, as said below
- embed_weight: float32 [32128, 1024], P(('shards', 'tensor', 'section')), may hold values from -6 to 6
- embed_grad: bfloat16 [32128, 1024], P(('shards', 'tensor', 'section')), may hold values from -6 to 6
- embed_moment: float32 [32128, 1024], P(('shards', 'tensor', 'section')), may hold values from -3 to 3
- embed_second: float32 [32128, 1024], P(('shards', 'tensor', 'section')), may hold values from 0.01 to 1
- norm_scale: float32 [16, 2048], P('section'), may hold values from 0.5 to 1.5
- norm_partial: float32 [16, 32, 2048], P('section', ('shards', 'tensor')), may hold values from -2 to 2
- norm_moment: float32 [16, 2048], P('section'), may hold values from -3 to 3
- norm_second: float32 [16, 2048], P('section'), may hold values from 0.01 to 0.5
- bias_table: float32 [32, 16], replicated, may hold values from -3 to 3
- bias_partial: float32 [128, 32, 16], P(('shards', 'tensor', 'section')), may hold values from -2 to 2
- bias_moment: float32 [32, 16], replicated, may hold values from -3 to 3
- bias_second: float32 [32, 16], replicated, may hold values from 0.01 to 1
Outputs:
- attn_momentum_new: bfloat16 [16, 4, 1024, 1024], P('section', None, 'shards', 'tensor')
- mlp_in_momentum_new: bfloat16 [16, 2, 1024, 2816], P('section', None, 'shards', 'tensor')
- mlp_out_momentum_new: bfloat16 [16, 2816, 1024], P('section', 'tensor', 'shards')
- attn_update: float32 [16, 4, 1024, 1024], P('section', None, 'shards', 'tensor')
- mlp_in_update: float32 [16, 2, 1024, 2816], P('section', None, 'shards', 'tensor')
- mlp_out_update: float32 [16, 2816, 1024], P('section', 'tensor', 'shards')
- owner_rms: float32 [128], P(('shards', 'tensor', 'section'))
- embed_weight_new: float32 [32128, 1024], P(('shards', 'tensor', 'section'))
- embed_moment_new: float32 [32128, 1024], P(('shards', 'tensor', 'section'))
- embed_second_new: float32 [32128, 1024], P(('shards', 'tensor', 'section'))
- norm_scale_new: float32 [16, 2048], P('section')
- norm_moment_new: float32 [16, 2048], P('section')
- norm_second_new: float32 [16, 2048], P('section')
- bias_table_new: float32 [32, 16], replicated
- bias_moment_new: float32 [32, 16], replicated
- bias_second_new: float32 [32, 16], replicated
Inputs may be any that keep to these rules, and one draw needn't show every extreme that they name: Owner o names the device of index o among the 32 devices of the layer's section, in the order of the mesh (shards first); the 28 matrices of the layers of one section have distinct owners, so a device owns at most one matrix.
All inputs are finite; a program needn't handle non-finite values.
Results may differ from a plain program's by a relative error of at most 0.018.
Values may be sent and summed in bfloat16 or wider, within the bound.
No kernel may reach another device: no remote copies, remote signals or barrier semaphores. Data moves between devices by JAX's collectives and lax.ppermute only.
A program may use at most 192 MiB of HBM per device.

v0:
```python
import math
import jax
import jax.numpy as jnp
from jax import lax
from jax.sharding import PartitionSpec as P

D = 1024
FF = 2816
NS_STEPS = 2
coef_first = 3.4445
coef_second = -4.775
coef_third = 2.0315


def orthogonalize(matrix):
    norm_value = jnp.sqrt(jnp.sum(matrix * matrix))
    current = (matrix / (norm_value + 1e-07)).astype(jnp.bfloat16)
    for sweep_index in range(NS_STEPS):
        gram_form = jnp.dot(current, current.T, preferred_element_type=jnp.float32).astype(
            jnp.bfloat16
        )
        square_form = jnp.dot(gram_form, gram_form, preferred_element_type=jnp.float32)
        polynomial = (
            coef_second * gram_form.astype(jnp.float32) + coef_third * square_form
        ).astype(jnp.bfloat16)
        current = (
            coef_first * current.astype(jnp.float32)
            + jnp.dot(polynomial, current, preferred_element_type=jnp.float32)
        ).astype(jnp.bfloat16)
    rms_value = norm_value / math.sqrt(matrix.shape[0] * matrix.shape[1])
    return (current, rms_value)


def zeroed(matrix):
    return (jnp.zeros(matrix.shape, jnp.bfloat16), jnp.zeros((), jnp.float32))


def refresh(gradient, moment):
    fresh_moment = (0.95 * moment.astype(jnp.float32) + gradient.astype(jnp.float32)).astype(
        jnp.bfloat16
    )
    advance = (gradient.astype(jnp.float32) + 0.95 * fresh_moment.astype(jnp.float32)).astype(
        jnp.bfloat16
    )
    return (fresh_moment, advance)


def adamw_update(weight, gradient, moment, second, decay_rate):
    moment_new = 0.9 * moment + 0.1 * gradient
    second_new = 0.95 * second + 0.05 * gradient * gradient
    weight_new = weight - 0.02 * (moment_new / (jnp.sqrt(second_new) + 1e-08) + decay_rate * weight)
    return (weight_new, moment_new, second_new)


def on_device(
    attn_grad,
    mlp_in_grad,
    mlp_out_grad,
    attn_momentum,
    mlp_in_momentum,
    mlp_out_momentum,
    owners,
    embed_weight,
    embed_grad,
    embed_moment,
    embed_second,
    norm_scale,
    norm_partial,
    norm_moment,
    norm_second,
    bias_table,
    bias_partial,
    bias_moment,
    bias_second,
):
    shards_count = lax.axis_size("shards")
    tensor_count = lax.axis_size("tensor")
    group_count = shards_count * tensor_count
    my_index = lax.axis_index(("shards", "tensor"))
    layers_here = owners.shape[0]
    rows_block = attn_grad.shape[2]
    cols_block = attn_grad.shape[3]
    ff_block = mlp_in_grad.shape[3]
    square_width = rows_block * cols_block
    rect_width = rows_block * ff_block
    attn_fresh, attn_ahead = refresh(attn_grad, attn_momentum)
    inner_fresh, inner_ahead = refresh(mlp_in_grad, mlp_in_momentum)
    outer_fresh, outer_ahead = refresh(mlp_out_grad, mlp_out_momentum)
    rect_ahead = jnp.concatenate([inner_ahead, jnp.swapaxes(outer_ahead, 1, 2)[:, None]], axis=1)
    slots = jnp.arange(group_count, dtype=jnp.int32)
    square_owner = owners[:, :4].reshape(-1)
    rect_owner = owners[:, 4:].reshape(-1)
    square_pick = (slots[:, None] == square_owner[None, :]).astype(jnp.bfloat16)
    rect_pick = (slots[:, None] == rect_owner[None, :]).astype(jnp.bfloat16)
    square_send = jnp.dot(
        square_pick,
        attn_ahead.reshape(layers_here * 4, square_width),
        preferred_element_type=jnp.float32,
    ).astype(jnp.bfloat16)
    rect_send = jnp.dot(
        rect_pick,
        rect_ahead.reshape(layers_here * 3, rect_width),
        preferred_element_type=jnp.float32,
    ).astype(jnp.bfloat16)
    outgoing = jnp.concatenate([square_send, rect_send], axis=1)
    incoming = lax.all_to_all(
        outgoing, ("shards", "tensor"), split_axis=0, concat_axis=0, tiled=True
    )
    square_in = incoming[:, :square_width]
    rect_in = incoming[:, square_width:]
    square_whole = (
        square_in.astype(jnp.float32)
        .reshape(shards_count, tensor_count, rows_block, cols_block)
        .transpose(0, 2, 1, 3)
        .reshape(shards_count * rows_block, tensor_count * cols_block)
    )
    rect_whole = (
        rect_in.astype(jnp.float32)
        .reshape(shards_count, tensor_count, rows_block, ff_block)
        .transpose(0, 2, 1, 3)
        .reshape(shards_count * rows_block, tensor_count * ff_block)
    )
    owns_square = jnp.any(square_owner == my_index)
    owns_rect = jnp.any(rect_owner == my_index)
    square_done, square_rms = lax.cond(owns_square, orthogonalize, zeroed, square_whole)
    rect_done, rect_rms = lax.cond(owns_rect, orthogonalize, zeroed, rect_whole)
    square_back = (
        square_done.reshape(shards_count, rows_block, tensor_count, cols_block)
        .transpose(0, 2, 1, 3)
        .reshape(group_count, square_width)
    )
    rect_back = (
        rect_done.reshape(shards_count, rows_block, tensor_count, ff_block)
        .transpose(0, 2, 1, 3)
        .reshape(group_count, rect_width)
    )
    returning = jnp.concatenate([square_back, rect_back], axis=1)
    arrived = lax.all_to_all(
        returning, ("shards", "tensor"), split_axis=0, concat_axis=0, tiled=True
    )
    square_arrived = arrived[:, :square_width]
    rect_arrived = arrived[:, square_width:]
    square_rows = jnp.take(square_arrived, square_owner, axis=0).reshape(
        layers_here, 4, rows_block, cols_block
    ).astype(jnp.float32) * (0.2 * math.sqrt(D))
    rect_rows = jnp.take(rect_arrived, rect_owner, axis=0).reshape(
        layers_here, 3, rows_block, ff_block
    ).astype(jnp.float32) * (0.2 * math.sqrt(FF))
    mlp_in_update = rect_rows[:, :2]
    mlp_out_update = jnp.swapaxes(rect_rows[:, 2], 1, 2)
    owner_rms = (square_rms + rect_rms).reshape(1)
    norm_grad = lax.psum(norm_partial[:, 0].astype(jnp.bfloat16), ("shards", "tensor")).astype(
        jnp.float32
    )
    bias_grad = lax.psum(bias_partial[0], ("shards", "tensor", "section"))
    embed_results = adamw_update(
        embed_weight, embed_grad.astype(jnp.float32), embed_moment, embed_second, 0.1
    )
    norm_results = adamw_update(norm_scale, norm_grad, norm_moment, norm_second, 0.0)
    bias_results = adamw_update(bias_table, bias_grad, bias_moment, bias_second, 0.0)
    return (
        attn_fresh,
        inner_fresh,
        outer_fresh,
        square_rows,
        mlp_in_update,
        mlp_out_update,
        owner_rms,
        embed_results[0],
        embed_results[1],
        embed_results[2],
        norm_results[0],
        norm_results[1],
        norm_results[2],
        bias_results[0],
        bias_results[1],
        bias_results[2],
    )


def solution(mesh):
    placed = (
        P("section", None, "shards", "tensor"),
        P("section", None, "shards", "tensor"),
        P("section", "tensor", "shards"),
        P("section", None, "shards", "tensor"),
        P("section", None, "shards", "tensor"),
        P("section", "tensor", "shards"),
        P("section", None),
        P(("shards", "tensor", "section"), None),
        P(("shards", "tensor", "section"), None),
        P(("shards", "tensor", "section"), None),
        P(("shards", "tensor", "section"), None),
        P("section", None),
        P("section", ("shards", "tensor"), None),
        P("section", None),
        P("section", None),
        P(),
        P(("shards", "tensor", "section"), None, None),
        P(),
        P(),
    )
    return jax.shard_map(
        on_device,
        mesh=mesh,
        in_specs=placed,
        out_specs=(
            P("section", None, "shards", "tensor"),
            P("section", None, "shards", "tensor"),
            P("section", "tensor", "shards"),
            P("section", None, "shards", "tensor"),
            P("section", None, "shards", "tensor"),
            P("section", "tensor", "shards"),
            P(("shards", "tensor", "section")),
            P(("shards", "tensor", "section"), None),
            P(("shards", "tensor", "section"), None),
            P(("shards", "tensor", "section"), None),
            P("section", None),
            P("section", None),
            P("section", None),
            P(),
            P(),
            P(),
        ),
        check_vma=False,
    )
```

profile of v0, /device:TPU:0, one launch (start us, length us, event | category | flops | bytes accessed | tf_op | source)
XLA Modules:
  0.0 756.0 jit_solution(7406743752380418459)
XLA Ops:
  2.3 3.1 fusion.16
  8.2 1.8 fusion.14
  10.2 2.6 copy.70
  12.9 5.0 reshape.176
  17.8 3.2 convolution_convert_fusion.1
  21.1 4.2 convolution_convert_fusion
  25.3 6.8 maximum_bitcast_fusion
  32.6 11.0 %reduce.4 = bf16[32,122880]{1,0:T(8,128)(2,1)} reduce(bf16[32,1,122880]{2,0,1:T(8,128)(2,1)} %maximum_bitcast_fusion, bf16[]{:T(256)} %broadcast.176), dimensions={1}, to_apply=%copy.71.reduce_sub_computation | reduce | bytes 15728642 | tf_op jit(solution)/shard_map/all_to_all | solution.py:106
  43.6 10.4 %reshape.205 = bf16[32,2,61440]{2,1,0:T(2,128)(2,1)} reshape(bf16[32,122880]{1,0:T(8,128)(2,1)} %reduce.4) | data formatting | bytes 15728640
  54.0 8.5 %all-to-all-start = ((bf16[32,2,61440]{2,1,0:T(2,128)(2,1)}), bf16[32,2,61440]{2,1,0:T(2,128)(2,1)}, u32[]{:S(2)}, u32[]{:S(2)}) async-start(bf16[32,2,61440]{2,1,0:T(2,128)(2,1)} %reshape.205), calls=%async_computation | async-start | bytes 15728640 | tf_op jit(solution)/shard_map/all_to_all | solution.py:106
  66.3 94.9 %all-to-all-done = bf16[32,2,61440]{2,1,0:T(2,128)(2,1)} async-done(((bf16[32,2,61440]{2,1,0:T(2,128)(2,1)}), bf16[32,2,61440]{2,1,0:T(2,128)(2,1)}, u32[]{:S(2)}, u32[]{:S(2)}) %all-to-all-start) | async-done | bytes 7864352 | tf_op jit(solution)/shard_map/all_to_all | solution.py:106
  161.2 23.7 %reshape.206 = bf16[32,1,122880]{2,1,0:T(2,128)(2,1)} reshape(bf16[32,2,61440]{2,1,0:T(2,128)(2,1)} %all-to-all-done) | data formatting | bytes 15728640
  184.9 17.1 %copy.103 = bf16[32,1,122880]{2,0,1:T(8,128)(2,1)} copy(bf16[32,1,122880]{2,1,0:T(2,128)(2,1)} %reshape.206) | data formatting | bytes 15728640
  202.0 1.9 slice_convert_fusion.1
  203.9 7.6 %slice_convert_fusion = f32[32,90112]{1,0:T(8,128)} fusion(bf16[32,122880]{1,0:T(8,128)(2,1)} %bitcast.90), kind=kLoop, calls=%fused_computation.31 | loop fusion | flops 2883584 | bytes 17301504 | tf_op jit(solution)/shard_map/transpose | solution.py:120
  212.8 4.8 copy.105
  217.6 36.5 %conditional.2 = (bf16[1024,1024]{1,0:T(8,128)(2,1)S(1)}, f32[]{:T(128)}) conditional(s32[]{:T(128)} %convert_element_type.167, () %tuple.24, f32[8,128,4,256]{3,2,1,0:T(4,128)} %bitcast.88), branch_computations={%region_1.0_spmd, %region_2.4_spmd} | conditional | flops 12907970560 | bytes 35651640 | solution.py:125
  217.6 4.9 multiply_reduce_fusion
  223.3 3.0 divide_convert_fusion
  226.7 3.7 fusion.38
  230.4 8.8 %add_convert_fusion.2 = bf16[1024,1024]{1,0:T(8,128)(2,1)} fusion(bf16[1024,1024]{1,0:T(8,128)(2,1)S(1)} %bitcast.108, bf16[1024,1024]{1,0:T(8,128)(2,1)} %fusion.38), kind=kOutput, calls=%fused_computation.4 | convolution fusion | flops 4304404480 | bytes 6291456 | tf_op jit(solution)/shard_map/cond/branch_1_fun/dot_general | solution.py:28
  239.2 5.9 fusion.39
  245.2 8.8 %add_convert_fusion = bf16[1024,1024]{1,0:T(8,128)(2,1)S(1)} fusion(bf16[1024,1024]{1,0:T(8,128)(2,1)} %add_convert_fusion.2, bf16[1024,1024]{1,0:T(8,128)(2,1)} %fusion.39), kind=kOutput, calls=%fused_computation.2 | convolution fusion | flops 4304404480 | bytes 6291456 | tf_op jit(solution)/shard_map/cond/branch_1_fun/dot_general | solution.py:28
  254.2 2.8 reshape.178
  256.9 2.0 copy.73
  260.1 12.1 %reshape.187 = f32[8,4,128,704]{3,2,1,0:T(8,128)} reshape(f32[32,90112]{1,0:T(8,128)} %slice_convert_fusion) | data formatting | bytes 23068672 | tf_op jit(solution)/shard_map/transpose | solution.py:120
  272.2 11.3 %conditional.3 = (bf16[1024,2816]{1,0:T(8,128)(2,1)}, f32[]{:T(128)}) conditional(s32[]{:T(128)} %convert_element_type.176, () %tuple.25, f32[8,128,4,704]{3,1,2,0:T(8,128)} %bitcast.87), branch_computations={%region_5.0_spmd, %region_6.0_spmd} | conditional | flops 27962376192 | bytes 174063744 | solution.py:126
  272.2 2.9 broadcast.120
  283.5 14.0 %reshape.204 = bf16[8,128,4,704]{3,2,1,0:T(4,128)(2,1)} reshape(bf16[1024,2816]{1,0:T(8,128)(2,1)} %get-tuple-element.25) | data formatting | bytes 11534336 | tf_op jit(solution)/shard_map/reshape | solution.py:133
  297.5 6.6 copy.104
  304.2 10.1 %reshape.182 = bf16[32,90112]{1,0:T(8,128)(2,1)} reshape(bf16[8,4,128,704]{3,2,1,0:T(8,128)(2,1)} %bitcast.93) | data formatting | bytes 11534336 | tf_op jit(solution)/shard_map/reshape | solution.py:135
  314.3 6.2 maximum_bitcast_fusion.1
  320.4 11.0 %reduce.5 = bf16[32,122880]{1,0:T(8,128)(2,1)} reduce(bf16[32,1,122880]{2,0,1:T(8,128)(2,1)} %maximum_bitcast_fusion.1, bf16[]{:T(256)} %broadcast.176), dimensions={1}, to_apply=%copy.77.reduce_sub_computation | reduce | bytes 15728642 | tf_op jit(solution)/shard_map/all_to_all | solution.py:138
  331.4 10.4 %reshape.207 = bf16[32,2,61440]{2,1,0:T(2,128)(2,1)} reshape(bf16[32,122880]{1,0:T(8,128)(2,1)} %reduce.5) | data formatting | bytes 15728640
  341.9 47.0 %all-to-all-start.1 = ((bf16[32,2,61440]{2,1,0:T(2,128)(2,1)}), bf16[32,2,61440]{2,1,0:T(2,128)(2,1)}, u32[]{:S(2)}, u32[]{:S(2)}) async-start(bf16[32,2,61440]{2,1,0:T(2,128)(2,1)} %reshape.207), calls=%async_computation.1 | async-start | bytes 15728640 | tf_op jit(solution)/shard_map/all_to_all | solution.py:138
  389.1 158.5 %psum.15 = f32[32,16]{0,1:T(8,128)S(1)} all-reduce(f32[32,16]{0,1:T(8,128)S(1)} %bitcast.112), channel_id=1, replica_groups=mesh['shards'=8,'tensor'=4,'section'=4] {'shards','tensor','section'}, use_global_device_ids=true, to_apply=%region_9.10 | all-reduce | flops 512 | bytes 4096 | tf_op jit(solution)/shard_map/psum | solution.py:155
  547.6 125.7 %psum.14 = bf16[4,2048]{1,0:T(4,128)(2,1)S(1)} all-reduce(bf16[4,2048]{1,0:T(4,128)(2,1)S(1)} %bitcast.109), channel_id=1, replica_groups=mesh['shards'=8,'tensor'=4,'section'=4] {'shards','tensor'}, use_global_device_ids=true, to_apply=%region_8.9 | all-reduce | flops 8192 | bytes 32768 | tf_op jit(solution)/shard_map/psum | solution.py:152
  674.0 3.2 multiply_subtract_fusion
  677.9 23.2 %reshape.208 = bf16[32,1,122880]{2,1,0:T(2,128)(2,1)} reshape(bf16[32,2,61440]{2,1,0:T(2,128)(2,1)} %all-to-all-done.1) | data formatting | bytes 15728640
  701.0 17.1 %copy.102 = bf16[32,1,122880]{2,0,1:T(8,128)(2,1)} copy(bf16[32,1,122880]{2,1,0:T(2,128)(2,1)} %reshape.208) | data formatting | bytes 15728640
  718.1 1.7 slice.38
  719.9 5.6 slice.39
  725.4 9.0 %gather_fusion.1 = bf16[12,90112]{1,0:T(8,128)(2,1)} fusion(bf16[32,90112]{1,0:T(8,128)(2,1)} %slice.39, s32[1024]{0:T(1024)S(1)} %pad_clamp_fusion), kind=kCustom, calls=%fused_computation.1 | custom fusion | bytes 4325424 | tf_op jit(solution)/shard_map/jit(_take)/gather | solution.py:146
  734.4 5.2 gather.15
  739.6 2.3 convert_multiply_fusion
  743.2 1.9 slice.40
  747.6 3.6 copy.79
  752.8 1.7 convert_multiply_fusion.1
  (72 shorter events, 17.4 us)
Async XLA Ops:
  1.4 5.5 copy-start.16
  2.3 4.7 copy-start.8
  2.3 4.7 copy-start.9
  5.4 2.8 copy-start.3
  5.4 2.8 copy-start.4
  54.0 8.5 %copy-start.10 = (s32[4,7]{1,0:T(4,128)S(1)}, s32[4,7]{1,0:T(4,128)}, u32[]{:S(2)}) copy-start(s32[4,7]{1,0:T(4,128)} %param.29) | copy-start | bytes 340
  54.0 107.2 %all-to-all-start = ((bf16[32,2,61440]{2,1,0:T(2,128)(2,1)}), bf16[32,2,61440]{2,1,0:T(2,128)(2,1)}, u32[]{:S(2)}, u32[]{:S(2)}) async-start(bf16[32,2,61440]{2,1,0:T(2,128)(2,1)} %reshape.205), calls=%async_computation | async-start | bytes 15728640 | tf_op jit(solution)/shard_map/all_to_all | solution.py:106
  341.8 47.0 %copy-start.11 = (s32[4,7]{1,0:T(4,128)S(1)}, s32[4,7]{1,0:T(4,128)}, u32[]{:S(2)}) copy-start(s32[4,7]{1,0:T(4,128)} %param.29) | copy-start | bytes 340
  341.8 47.1 %copy-start.17 = (s32[4,3]{1,0:T(4,128)S(1)}, s32[4,3]{1,0:T(4,128)}, u32[]{:S(2)}) copy-start(s32[4,3]{1,0:T(4,128)} %copy-done.16) | copy-start | bytes 148
  341.8 47.2 %copy-start.12 = (f32[4,1,2048]{2,1,0:T(1,128)S(1)}, f32[4,1,2048]{2,1,0:T(1,128)}, u32[]{:S(2)}) copy-start(f32[4,1,2048]{2,1,0:T(1,128)} %param.35) | copy-start | bytes 98308
  341.8 47.2 %copy-start.21 = (f32[1,32,16]{1,2,0:T(8,128)S(1)}, f32[1,32,16]{1,2,0:T(8,128)}, u32[]{:S(2)}) copy-start(f32[1,32,16]{1,2,0:T(8,128)} %param.39) | copy-start | bytes 6148
  341.8 331.4 %copy-start.18 = (f32[32,16]{0,1:T(8,128)S(1)}, f32[32,16]{0,1:T(8,128)}, u32[]{:S(2)}) copy-start(f32[32,16]{0,1:T(8,128)} %param.38) | copy-start | bytes 6148
  341.8 331.4 %copy-start.19 = (f32[32,16]{0,1:T(8,128)S(1)}, f32[32,16]{0,1:T(8,128)}, u32[]{:S(2)}) copy-start(f32[32,16]{0,1:T(8,128)} %param.41) | copy-start | bytes 6148
  341.9 331.4 %copy-start.20 = (f32[32,16]{0,1:T(8,128)S(1)}, f32[32,16]{0,1:T(8,128)}, u32[]{:S(2)}) copy-start(f32[32,16]{0,1:T(8,128)} %param.40) | copy-start | bytes 6148
  341.9 332.1 %copy-start.5 = (f32[251,1024]{1,0:T(8,128)S(1)}, f32[251,1024]{1,0:T(8,128)}, u32[]{:S(2)}) copy-start(f32[251,1024]{1,0:T(8,128)} %param.30) | copy-start | bytes 3084292
  341.9 332.1 %copy-start.6 = (f32[251,1024]{1,0:T(8,128)S(1)}, f32[251,1024]{1,0:T(8,128)}, u32[]{:S(2)}) copy-start(f32[251,1024]{1,0:T(8,128)} %param.33) | copy-start | bytes 3084292
  341.9 332.0 %copy-start.7 = (f32[251,1024]{1,0:T(8,128)S(1)}, f32[251,1024]{1,0:T(8,128)}, u32[]{:S(2)}) copy-start(f32[251,1024]{1,0:T(8,128)} %param.32) | copy-start | bytes 3084292
  341.9 335.9 %all-to-all-start.1 = ((bf16[32,2,61440]{2,1,0:T(2,128)(2,1)}), bf16[32,2,61440]{2,1,0:T(2,128)(2,1)}, u32[]{:S(2)}, u32[]{:S(2)}) async-start(bf16[32,2,61440]{2,1,0:T(2,128)(2,1)} %reshape.207), calls=%async_computation.1 | async-start | bytes 15728640 | tf_op jit(solution)/shard_map/all_to_all | solution.py:138
  673.9 3.2 copy-start.13
  674.0 3.2 copy-start.14
  674.0 3.2 copy-start.15
  734.4 5.2 copy-start.22
  747.6 3.6 copy-start.1
  747.6 5.2 copy-start.2
  747.6 5.2 copy-start.23
where the time goes:
time: 762 us; the launch traced here: 756 us
  blocking collectives  284 us (37%)
  local copies, waits for them, and re-layouts  204 us (27%)
  waiting for transfers between devices  94.9 us (12%)
  other arithmetic  69.7 us (9%)
  starting transfers between devices  55.5 us (7%)
  matrix products  34.6 us (5%)
  loops' own time  9.38 us (1%)
    psum x1, blocking collectives, on_device(): bias_grad = lax.psum(bias_partial[0], ('shards', 'tensor', 'section'))  159 us
    psum x1, blocking collectives, on_device(): lax.psum(norm_partial[:, 0].astype(jnp.bfloat16), ('shards', 'tensor'))  126 us
    unnamed x59, local copies, waits for them, and re-layouts  112 us
    all_to_all x1, waiting for transfers between devices, on_device(): lax.all_to_all(outgoing, ('shards', 'tensor'), split_axis=0, concat_axis=...  94.9 us
    all_to_all x1, starting transfers between devices, on_device(): lax.all_to_all(returning, ('shards', 'tensor'), split_axis=0, concat_axis...  47 us
    all_to_all x2, other arithmetic, on_device(): lax.all_to_all(outgoing, ('shards', 'tensor'), split_axis=0, concat_axis=...  17.8 us
    dot_general x2, matrix products, orthogonalize(): jnp.dot(polynomial, current, preferred_element_type=jnp.float32)  17.6 us
    all_to_all x2, other arithmetic, on_device(): lax.all_to_all(returning, ('shards', 'tensor'), split_axis=0, concat_axis...  17.2 us
  transfers between devices with their start and end apart: 2, of which 1 were waited for; matrix products, arithmetic and copies ran while one was open for 1% of the time, Pallas kernels for 0%

commit v1 on v0

--- a/solution.py
+++ b/solution.py
@@ -10,6 +10,11 @@
 coef_first = 3.4445
 coef_second = -4.775
 coef_third = 2.0315
+
+
+def summed_here(block, axis):
+    parts = lax.all_gather(block, axis)
+    return jnp.sum(parts, axis=0)
 
 
 def orthogonalize(matrix):
@@ -149,7 +154,7 @@
     mlp_in_update = rect_rows[:, :2]
     mlp_out_update = jnp.swapaxes(rect_rows[:, 2], 1, 2)
     owner_rms = (square_rms + rect_rms).reshape(1)
-    norm_grad = lax.psum(norm_partial[:, 0].astype(jnp.bfloat16), ("shards", "tensor")).astype(
+    norm_grad = summed_here(norm_partial[:, 0].astype(jnp.bfloat16), ("shards", "tensor")).astype(
         jnp.float32
     )
     bias_grad = lax.psum(bias_partial[0], ("shards", "tensor", "section"))

time: 762 us -> 684 us (0.90)
  blocking collectives: 284 us -> 202 us
    all_gather x0 -> x1, blocking collectives: none -> 136 us  [summed_here(): parts = lax.all_gather(block, axis)]
    psum x1 -> x0, blocking collectives: 126 us -> none  [on_device(): lax.psum(norm_partial[:, 0].astype(jnp.bfloat16), ('shards', 'tensor'))]
    psum x1, blocking collectives: 159 us -> 65.6 us  [on_device(): bias_grad = lax.psum(bias_partial[0], ('shards', 'tensor', 'section'))]
    unnamed x59 -> x56, local copies, waits for them, and re-layouts: 112 us -> 113 us
  transfers between devices with their start and end apart: 2 -> 2, of which waited for: 1 -> 1; matrix products, arithmetic and copies ran while one was open for 1% -> 2% of each run, Pallas kernels for 0% -> 0%
where the time goes in v1:
time: 684 us; the launch traced here: 677 us
  local copies, waits for them, and re-layouts  204 us (30%)
  blocking collectives  202 us (30%)
  waiting for transfers between devices  94.9 us (14%)
  other arithmetic  73.5 us (11%)
  starting transfers between devices  54.9 us (8%)
  matrix products  34.6 us (5%)
  loops' own time  9.34 us (1%)
    all_gather x1, blocking collectives, summed_here(): parts = lax.all_gather(block, axis)  136 us
    unnamed x56, local copies, waits for them, and re-layouts  113 us
    all_to_all x1, waiting for transfers between devices, on_device(): lax.all_to_all(outgoing, ('shards', 'tensor'), split_axis=0, concat_axis=...  94.9 us
    psum x1, blocking collectives, on_device(): bias_grad = lax.psum(bias_partial[0], ('shards', 'tensor', 'section'))  65.6 us
    all_to_all x1, starting transfers between devices, on_device(): lax.all_to_all(returning, ('shards', 'tensor'), split_axis=0, concat_axis...  46.3 us
    all_to_all x2, other arithmetic, on_device(): lax.all_to_all(outgoing, ('shards', 'tensor'), split_axis=0, concat_axis=...  17.8 us
    dot_general x2, matrix products, orthogonalize(): jnp.dot(polynomial, current, preferred_element_type=jnp.float32)  17.6 us
    all_to_all x2, other arithmetic, on_device(): lax.all_to_all(returning, ('shards', 'tensor'), split_axis=0, concat_axis...  17.1 us
  transfers between devices with their start and end apart: 2, of which 1 were waited for; matrix products, arithmetic and copies ran while one was open for 2% of the time, Pallas kernels for 0%

profile of v1, /device:TPU:0, one launch (start us, length us, event | category | flops | bytes accessed | tf_op | source)
XLA Modules:
  0.0 677.2 jit_solution(14850803662192914981)
XLA Ops:
  2.3 3.1 fusion.16
  8.2 1.8 fusion.14
  10.2 2.7 copy.67
  12.9 5.0 reshape.186
  17.9 3.2 convolution_convert_fusion.1
  21.1 4.2 convolution_convert_fusion
  25.3 6.9 %maximum_bitcast_fusion = bf16[32,1,122880]{2,0,1:T(8,128)(2,1)} fusion(bf16[32,90112]{1,0:T(8,128)(2,1)} %convolution_convert_fusion, bf16[32,32768]{1,0:T(8,128)(2,1)} %convolution_convert_fusion.1), kind=kLoop, calls=%fused_computation.26 | loop fusion | flops 15728640 | bytes 15728640 | tf_op jit(solution)/shard_map/all_to_all | solution.py:111
  32.7 11.0 %reduce.6 = bf16[32,122880]{1,0:T(8,128)(2,1)} reduce(bf16[32,1,122880]{2,0,1:T(8,128)(2,1)} %maximum_bitcast_fusion, bf16[]{:T(256)} %broadcast.177), dimensions={1}, to_apply=%copy.68.reduce_sub_computation | reduce | bytes 15728642 | tf_op jit(solution)/shard_map/all_to_all | solution.py:111
  43.6 10.4 %reshape.217 = bf16[32,2,61440]{2,1,0:T(2,128)(2,1)} reshape(bf16[32,122880]{1,0:T(8,128)(2,1)} %reduce.6) | data formatting | bytes 15728640
  54.0 8.6 %all-to-all-start = ((bf16[32,2,61440]{2,1,0:T(2,128)(2,1)}), bf16[32,2,61440]{2,1,0:T(2,128)(2,1)}, u32[]{:S(2)}, u32[]{:S(2)}) async-start(bf16[32,2,61440]{2,1,0:T(2,128)(2,1)} %reshape.217), calls=%async_computation | async-start | bytes 15728640 | tf_op jit(solution)/shard_map/all_to_all | solution.py:111
  66.4 94.9 %all-to-all-done = bf16[32,2,61440]{2,1,0:T(2,128)(2,1)} async-done(((bf16[32,2,61440]{2,1,0:T(2,128)(2,1)}), bf16[32,2,61440]{2,1,0:T(2,128)(2,1)}, u32[]{:S(2)}, u32[]{:S(2)}) %all-to-all-start) | async-done | bytes 7864352 | tf_op jit(solution)/shard_map/all_to_all | solution.py:111
  161.3 23.7 %reshape.218 = bf16[32,1,122880]{2,1,0:T(2,128)(2,1)} reshape(bf16[32,2,61440]{2,1,0:T(2,128)(2,1)} %all-to-all-done) | data formatting | bytes 15728640
  185.1 17.1 %copy.97 = bf16[32,1,122880]{2,0,1:T(8,128)(2,1)} copy(bf16[32,1,122880]{2,1,0:T(2,128)(2,1)} %reshape.218) | data formatting | bytes 15728640
  202.2 1.9 slice_convert_fusion.1
  204.1 7.6 %slice_convert_fusion = f32[32,90112]{1,0:T(8,128)} fusion(bf16[32,122880]{1,0:T(8,128)(2,1)} %bitcast.87), kind=kLoop, calls=%fused_computation.31 | loop fusion | flops 2883584 | bytes 17301504 | tf_op jit(solution)/shard_map/transpose | solution.py:125
  213.0 4.8 copy.99
  217.8 36.5 %conditional.2 = (bf16[1024,1024]{1,0:T(8,128)(2,1)S(1)}, f32[]{:T(128)}) conditional(s32[]{:T(128)} %convert_element_type.176, () %tuple.24, f32[8,128,4,256]{3,2,1,0:T(4,128)} %bitcast.85), branch_computations={%region_1.0_spmd, %region_2.4_spmd} | conditional | flops 12907970560 | bytes 35651640 | solution.py:130
  217.8 4.9 multiply_reduce_fusion
  223.4 3.0 divide_convert_fusion
  226.9 3.7 fusion.37
  230.6 8.8 %add_convert_fusion.2 = bf16[1024,1024]{1,0:T(8,128)(2,1)} fusion(bf16[1024,1024]{1,0:T(8,128)(2,1)S(1)} %bitcast.105, bf16[1024,1024]{1,0:T(8,128)(2,1)} %fusion.37), kind=kOutput, calls=%fused_computation.4 | convolution fusion | flops 4304404480 | bytes 6291456 | tf_op jit(solution)/shard_map/cond/branch_1_fun/dot_general | solution.py:33
  239.4 5.9 fusion.38
  245.3 8.8 %add_convert_fusion = bf16[1024,1024]{1,0:T(8,128)(2,1)S(1)} fusion(bf16[1024,1024]{1,0:T(8,128)(2,1)} %add_convert_fusion.2, bf16[1024,1024]{1,0:T(8,128)(2,1)} %fusion.38), kind=kOutput, calls=%fused_computation.2 | convolution fusion | flops 4304404480 | bytes 6291456 | tf_op jit(solution)/shard_map/cond/branch_1_fun/dot_general | solution.py:33
  254.3 2.8 reshape.188
  257.1 2.0 copy.70
  260.3 12.1 %reshape.197 = f32[8,4,128,704]{3,2,1,0:T(8,128)} reshape(f32[32,90112]{1,0:T(8,128)} %slice_convert_fusion) | data formatting | bytes 23068672 | tf_op jit(solution)/shard_map/transpose | solution.py:125
  272.3 11.3 %conditional.3 = (bf16[1024,2816]{1,0:T(8,128)(2,1)}, f32[]{:T(128)}) conditional(s32[]{:T(128)} %convert_element_type.185, () %tuple.25, f32[8,128,4,704]{3,1,2,0:T(8,128)} %bitcast.84), branch_computations={%region_5.0_spmd, %region_6.0_spmd} | conditional | flops 27962376192 | bytes 174063744 | solution.py:131
  272.3 2.9 broadcast.120
  283.6 14.0 %reshape.215 = bf16[8,128,4,704]{3,2,1,0:T(4,128)(2,1)} reshape(bf16[1024,2816]{1,0:T(8,128)(2,1)} %get-tuple-element.25) | data formatting | bytes 11534336 | tf_op jit(solution)/shard_map/reshape | solution.py:138
  297.6 6.6 copy.98
  304.3 10.1 %reshape.192 = bf16[32,90112]{1,0:T(8,128)(2,1)} reshape(bf16[8,4,128,704]{3,2,1,0:T(8,128)(2,1)} %bitcast.90) | data formatting | bytes 11534336 | tf_op jit(solution)/shard_map/reshape | solution.py:140
  314.3 6.2 maximum_bitcast_fusion.1
  320.5 11.0 %reduce.7 = bf16[32,122880]{1,0:T(8,128)(2,1)} reduce(bf16[32,1,122880]{2,0,1:T(8,128)(2,1)} %maximum_bitcast_fusion.1, bf16[]{:T(256)} %broadcast.177), dimensions={1}, to_apply=%copy.74.reduce_sub_computation | reduce | bytes 15728642 | tf_op jit(solution)/shard_map/all_to_all | solution.py:143
  331.5 10.4 %reshape.219 = bf16[32,2,61440]{2,1,0:T(2,128)(2,1)} reshape(bf16[32,122880]{1,0:T(8,128)(2,1)} %reduce.7) | data formatting | bytes 15728640
  341.9 46.3 %all-to-all-start.1 = ((bf16[32,2,61440]{2,1,0:T(2,128)(2,1)}), bf16[32,2,61440]{2,1,0:T(2,128)(2,1)}, u32[]{:S(2)}, u32[]{:S(2)}) async-start(bf16[32,2,61440]{2,1,0:T(2,128)(2,1)} %reshape.219), calls=%async_computation.1 | async-start | bytes 15728640 | tf_op jit(solution)/shard_map/all_to_all | solution.py:143
  388.5 136.2 %all-gather = bf16[128,1,2048]{2,1,0:T(2,128)(2,1)S(1)} all-gather(bf16[4,1,2048]{2,1,0:T(2,128)(2,1)S(1)} %convert_element_type.189), channel_id=2, replica_groups=mesh['shards'=8,'tensor'=4,'section'=4] {'shards','tensor'}, dimensions={0}, use_global_device_ids=true | all-gather | bytes 540672 | tf_op jit(solution)/shard_map/all_gather | solution.py:16
  524.8 3.1 reduce.5
  528.3 65.6 %psum.7 = f32[32,16]{0,1:T(8,128)S(1)} all-reduce(f32[32,16]{0,1:T(8,128)S(1)} %bitcast.108), channel_id=1, replica_groups=mesh['shards'=8,'tensor'=4,'section'=4] {'shards','tensor','section'}, use_global_device_ids=true, to_apply=%region_9.10 | all-reduce | flops 512 | bytes 4096 | tf_op jit(solution)/shard_map/psum | solution.py:160
  594.6 3.7 multiply_subtract_fusion
  599.0 23.6 %reshape.220 = bf16[32,1,122880]{2,1,0:T(2,128)(2,1)} reshape(bf16[32,2,61440]{2,1,0:T(2,128)(2,1)} %all-to-all-done.1) | data formatting | bytes 15728640
  622.6 17.1 %copy.96 = bf16[32,1,122880]{2,0,1:T(8,128)(2,1)} copy(bf16[32,1,122880]{2,1,0:T(2,128)(2,1)} %reshape.220) | data formatting | bytes 15728640
  639.7 1.7 slice.38
  641.4 5.6 slice.39
  647.0 8.9 %gather_fusion.1 = bf16[12,90112]{1,0:T(8,128)(2,1)} fusion(bf16[32,90112]{1,0:T(8,128)(2,1)} %slice.39, s32[1024]{0:T(1024)S(1)} %pad_clamp_fusion), kind=kCustom, calls=%fused_computation.1 | custom fusion | bytes 4325424 | tf_op jit(solution)/shard_map/jit(_take)/gather | solution.py:151
  656.0 5.2 gather.15
  661.1 2.3 convert_multiply_fusion
  664.7 1.9 slice.40
  669.1 3.6 copy.75
  (73 shorter events, 19.5 us)
Async XLA Ops:
  1.4 5.5 copy-start.15
  2.3 4.7 copy-start.6
  2.3 4.7 copy-start.7
  5.4 2.8 copy-start.3
  5.4 2.8 copy-start.4
  54.0 8.6 %copy-start.9 = (s32[4,7]{1,0:T(4,128)S(1)}, s32[4,7]{1,0:T(4,128)}, u32[]{:S(2)}) copy-start(s32[4,7]{1,0:T(4,128)} %param.29) | copy-start | bytes 340
  54.0 107.3 %all-to-all-start = ((bf16[32,2,61440]{2,1,0:T(2,128)(2,1)}), bf16[32,2,61440]{2,1,0:T(2,128)(2,1)}, u32[]{:S(2)}, u32[]{:S(2)}) async-start(bf16[32,2,61440]{2,1,0:T(2,128)(2,1)} %reshape.217), calls=%async_computation | async-start | bytes 15728640 | tf_op jit(solution)/shard_map/all_to_all | solution.py:111
  341.9 46.4 %copy-start.10 = (s32[4,7]{1,0:T(4,128)S(1)}, s32[4,7]{1,0:T(4,128)}, u32[]{:S(2)}) copy-start(s32[4,7]{1,0:T(4,128)} %param.29) | copy-start | bytes 340
  341.9 46.5 %copy-start.16 = (s32[4,3]{1,0:T(4,128)S(1)}, s32[4,3]{1,0:T(4,128)}, u32[]{:S(2)}) copy-start(s32[4,3]{1,0:T(4,128)} %copy-done.15) | copy-start | bytes 148
  341.9 46.6 %copy-start.11 = (f32[4,1,2048]{2,1,0:T(1,128)S(1)}, f32[4,1,2048]{2,1,0:T(1,128)}, u32[]{:S(2)}) copy-start(f32[4,1,2048]{2,1,0:T(1,128)} %param.35) | copy-start | bytes 98308
  341.9 257.1 %all-to-all-start.1 = ((bf16[32,2,61440]{2,1,0:T(2,128)(2,1)}), bf16[32,2,61440]{2,1,0:T(2,128)(2,1)}, u32[]{:S(2)}, u32[]{:S(2)}) async-start(bf16[32,2,61440]{2,1,0:T(2,128)(2,1)} %reshape.219), calls=%async_computation.1 | async-start | bytes 15728640 | tf_op jit(solution)/shard_map/all_to_all | solution.py:143
  388.3 140.0 %copy-start.20 = (f32[1,32,16]{1,2,0:T(8,128)S(1)}, f32[1,32,16]{1,2,0:T(8,128)}, u32[]{:S(2)}) copy-start(f32[1,32,16]{1,2,0:T(8,128)} %param.39) | copy-start | bytes 6148
  388.3 205.7 %copy-start.17 = (f32[32,16]{0,1:T(8,128)S(1)}, f32[32,16]{0,1:T(8,128)}, u32[]{:S(2)}) copy-start(f32[32,16]{0,1:T(8,128)} %param.38) | copy-start | bytes 6148
  388.3 205.7 %copy-start.18 = (f32[32,16]{0,1:T(8,128)S(1)}, f32[32,16]{0,1:T(8,128)}, u32[]{:S(2)}) copy-start(f32[32,16]{0,1:T(8,128)} %param.41) | copy-start | bytes 6148
  388.3 205.7 %copy-start.19 = (f32[32,16]{0,1:T(8,128)S(1)}, f32[32,16]{0,1:T(8,128)}, u32[]{:S(2)}) copy-start(f32[32,16]{0,1:T(8,128)} %param.40) | copy-start | bytes 6148
  388.3 206.3 %copy-start.5 = (f32[251,1024]{1,0:T(8,128)S(1)}, f32[251,1024]{1,0:T(8,128)}, u32[]{:S(2)}) copy-start(f32[251,1024]{1,0:T(8,128)} %param.30) | copy-start | bytes 3084292
  388.3 206.3 %copy-start.8 = (bf16[251,1024]{1,0:T(8,128)(2,1)S(1)}, bf16[251,1024]{1,0:T(8,128)(2,1)}, u32[]{:S(2)}) copy-start(bf16[251,1024]{1,0:T(8,128)(2,1)} %param.31) | copy-start | bytes 1542148
  594.6 3.7 copy-start.12
  594.6 3.7 copy-start.13
  594.6 3.7 copy-start.14
  656.0 5.2 copy-start.21
  669.1 3.6 copy-start.1
  669.1 5.2 copy-start.2
  669.1 5.2 copy-start.22
